TPU v7x, 32 devices: a whole 2x2x4 slice. The times are simulated.
32 devices in a mesh: heads: 4 (over y, core), seq: 8 (over z, x).
Axes of the slice: x: 2, y: 2, z: 4, core: 2. Of those that a mesh axis runs over, the one named last changes fastest.
Arguments:
- hidden: bfloat16 [8, 256, 2048], P('seq', 'heads'), may hold values from -6 to 6
- norm_gain: bfloat16 [2048], replicated, may hold values from 0.099609375 to 1.8984375
- router_weight: bfloat16 [2048, 4], replicated, may hold values from -0.125 to 0.125
- att_experts: int32 [8, 256, 2], P('seq'), may hold values from 0 to 3, all different within a row
- q_weight: bfloat16 [4, 2048, 1024], P(None, None, 'heads'), may hold values from -0.125 to 0.125
- kv_weight: bfloat16 [2, 2048, 1024], P(None, None, 'heads'), may hold values from -0.125 to 0.125
- o_weight: bfloat16 [4, 1024, 2048], P(None, 'heads'), may hold values from -1 to 1
- kv_cache: bfloat16 [2, 128, 128, 1024], P(None, 'seq', None, 'heads'), may hold values from -200 to 200
- cached_blocks: int32 [8], replicated, may hold values from 1 to 32, 128 in all
- tail_trim: int32 [8], replicated, may hold values from 0 to 127
- block_pool: int32 [128], replicated, may hold values from 0 to 127, each once
Outputs:
- attn_out: bfloat16 [8, 256, 2048], P('seq', 'heads')
Inputs may be any that keep to these rules, and one draw needn't show every extreme that they name: `block_pool`: the cached_blocks sum to 128, so every block belongs to one request.
All inputs are finite; a program needn't handle non-finite values.
Results may differ from a plain program's by a relative error of at most 0.019.
The roundings to bfloat16 on the way count: a program that leaves them out, or rounds other values in their place, can miss the bound.
Values may be sent and summed in bfloat16 or wider, within the bound.
No kernel may reach another device: no remote copies, remote signals or barrier semaphores. Data moves between devices by JAX's collectives and lax.ppermute only.
A program may use at most 128 MiB of HBM per device.

v0:
```python
import functools
import numpy as np
import jax
import jax.numpy as jnp
from jax import lax
from jax.sharding import PartitionSpec as P

HD = 128
NEG_FILL = -1e30


def rotate(values, positions):
    half_dim = values.shape[-1] // 2
    inverse = 10000.0 ** (-2.0 * jnp.arange(half_dim, dtype=jnp.float32) / values.shape[-1])
    angles = positions.astype(jnp.float32)[:, None] * inverse[None, :]
    target = (values.shape[0],) + (1,) * (values.ndim - 2) + (half_dim,)
    cosine = jnp.cos(angles).reshape(target)
    sine_part = jnp.sin(angles).reshape(target)
    leading_part = values[..., :half_dim]
    trailing_part = values[..., half_dim:]
    return jnp.concatenate(
        [
            leading_part * cosine - trailing_part * sine_part,
            trailing_part * cosine + leading_part * sine_part,
        ],
        axis=-1,
    )


def normalize(rows, norm_gain):
    wide_rows = rows.astype(jnp.float32)
    scaled = wide_rows * lax.rsqrt(jnp.mean(wide_rows * wide_rows, axis=-1, keepdims=True) + 1e-05)
    return (scaled * norm_gain.astype(jnp.float32)).astype(jnp.bfloat16)


def route(normed, router_weight, chosen):
    logits = jnp.dot(normed, router_weight, preferred_element_type=jnp.float32)
    experts_all = router_weight.shape[1]
    onehot = (chosen[:, :, None] == jnp.arange(experts_all, dtype=jnp.int32)[None, None, :]).astype(
        jnp.float32
    )
    picked = jnp.sum(onehot * logits[:, None, :], axis=-1)
    return (onehot, jax.nn.softmax(picked, axis=-1))


def split_bf16(x):
    hi = lax.reduce_precision(x, exponent_bits=8, mantissa_bits=7)
    lo = lax.reduce_precision(x - hi, exponent_bits=8, mantissa_bits=7)
    return (hi, lo)


def seq_cycle(mesh):
    size = mesh.shape["seq"]
    plain = list(range(size))
    try:
        devices = np.moveaxis(np.asarray(mesh.devices), mesh.axis_names.index("seq"), -1)
        line = devices.reshape(-1, size)[0]
        coords = np.array([list(d.coords) for d in line])
    except Exception:
        return plain
    varying = [k for k in range(coords.shape[1]) if len(set(coords[:, k])) > 1]
    if len(varying) == 1:
        order = sorted(plain, key=lambda j: coords[j, varying[0]])
        return order[0::2] + order[1::2][::-1]
    if len(varying) != 2:
        return plain
    dim_a, dim_b = varying
    values_a = sorted(set(coords[:, dim_a]))
    values_b = sorted(set(coords[:, dim_b]))
    if len(values_a) % 2:
        dim_a, dim_b, values_a, values_b = (dim_b, dim_a, values_b, values_a)
    if len(values_a) % 2 or len(values_a) * len(values_b) != size:
        return plain
    at = {(coords[j, dim_a], coords[j, dim_b]): j for j in plain}
    cycle = [at[a, values_b[0]] for a in values_a]
    for row, a in enumerate(reversed(values_a)):
        columns = values_b[1:] if row % 2 == 0 else values_b[1:][::-1]
        cycle += [at[a, b] for b in columns]
    if sorted(cycle) != plain:
        return plain
    return cycle


def shift_all_gather(piece, axis_name):
    size = lax.axis_size(axis_name)
    rank = lax.axis_index(axis_name)
    by_offset = [piece] + [
        lax.ppermute(piece, axis_name, [(i, (i + s) % size) for i in range(size)])
        for s in range(1, size)
    ]
    by_offset = jnp.stack(by_offset[:1] + by_offset[1:][::-1], axis=0)
    return jnp.take(by_offset, (jnp.arange(size, dtype=jnp.int32) - rank) % size, axis=0)


def shift_reduce_scatter(rows, axis_name):
    size = lax.axis_size(axis_name)
    rank = lax.axis_index(axis_name)
    share = rows.shape[0] // size
    total = lax.dynamic_slice_in_dim(rows, rank * share, share, 0).astype(jnp.float32)
    for s in range(1, size):
        piece = lax.dynamic_slice_in_dim(rows, (rank + s) % size * share, share, 0)
        moved = lax.ppermute(piece, axis_name, [(i, (i + s) % size) for i in range(size)])
        total = total + moved.astype(jnp.float32)
    return total


def ring_all_gather(piece, axis_name, cycle):
    size = len(cycle)
    forward = [(cycle[i], cycle[(i + 1) % size]) for i in range(size)]
    backward = [(cycle[(i + 1) % size], cycle[i]) for i in range(size)]
    ahead = size // 2
    behind = size - 1 - ahead
    from_behind, from_ahead = ([], [])
    moving = piece
    for _ in range(ahead):
        moving = lax.ppermute(moving, axis_name, forward)
        from_behind.append(moving)
    moving = piece
    for _ in range(behind):
        moving = lax.ppermute(moving, axis_name, backward)
        from_ahead.append(moving)
    return jnp.stack([piece] + from_ahead + from_behind[::-1], axis=0)


def per_device(
    cycle,
    hidden,
    norm_gain,
    router_weight,
    att_experts,
    q_weight,
    kv_weight,
    o_weight,
    kv_cache,
    cached_blocks,
    tail_trim,
    block_pool,
):
    head_count = lax.axis_size("heads")
    seq_rank = lax.axis_index("seq")
    block_size = kv_cache.shape[2]
    local_blocks = kv_cache.shape[1]
    local_heads = q_weight.shape[2] // HD
    scale_q = HD ** (-0.5)
    normed = normalize(hidden[0], norm_gain)
    gathered = lax.all_gather(normed, "heads", axis=0, tiled=True)
    new_count = gathered.shape[0]
    chosen = att_experts[0]
    cached_len = cached_blocks * block_size - tail_trim
    positions = cached_len[seq_rank] + jnp.arange(new_count, dtype=jnp.int32)
    onehot, gates = route(gathered, router_weight, chosen)
    every_q = jnp.einsum("nd,edc->nec", gathered, q_weight, preferred_element_type=jnp.float32)
    chosen_q = jnp.sum(onehot[:, :, :, None] * every_q[:, None, :, :], axis=2).reshape(
        new_count, 2, local_heads, HD
    )
    queries = rotate(chosen_q, positions).astype(jnp.bfloat16)
    fresh = jnp.einsum("nd,sdc->snc", gathered, kv_weight, preferred_element_type=jnp.float32)
    new_keys = rotate(fresh[0].reshape(new_count, local_heads, HD), positions).astype(jnp.bfloat16)
    new_values = fresh[1].reshape(new_count, local_heads, HD).astype(jnp.bfloat16)
    ring_queries = ring_all_gather(queries, "seq", cycle)
    request_count = ring_queries.shape[0]
    ring_size = len(cycle)
    position_of = np.argsort(np.asarray(cycle))
    position = jnp.asarray(position_of, dtype=jnp.int32)[seq_rank]
    pool_size = block_pool.shape[0]
    global_ids = seq_rank * local_blocks + jnp.arange(local_blocks, dtype=jnp.int32)
    matches = block_pool[None, :] == global_ids[:, None]
    slot_of = jnp.sum(
        jnp.where(matches, jnp.arange(pool_size, dtype=jnp.int32)[None, :], 0), axis=1
    )
    starts = jnp.cumsum(cached_blocks) - cached_blocks
    owner = jnp.sum((starts[None, :] <= slot_of[:, None]).astype(jnp.int32), axis=1) - 1
    ordinal = slot_of - starts[owner]
    owns = owner[None, :] == jnp.arange(request_count, dtype=jnp.int32)[:, None]
    self_scores = (
        jnp.einsum("nkhc,thc->hnkt", queries, new_keys, preferred_element_type=jnp.float32)
        * scale_q
    )
    causal = (
        jnp.arange(new_count, dtype=jnp.int32)[None, :]
        <= jnp.arange(new_count, dtype=jnp.int32)[:, None]
    )
    self_scores = jnp.where(causal[None, :, None, :], self_scores, NEG_FILL)
    self_best = jnp.max(self_scores, axis=-1)
    self_weights = jnp.exp(self_scores - self_best[..., None])
    self_total = jnp.sum(self_weights, axis=-1)
    self_accum = jnp.einsum(
        "hnkt,thc->hnkc",
        self_weights.astype(jnp.bfloat16),
        new_values,
        preferred_element_type=jnp.float32,
    )
    ring_queries, self_best, self_total, self_accum = lax.optimization_barrier(
        (ring_queries, self_best, self_total, self_accum)
    )
    owner_offset = (jnp.asarray(position_of, dtype=jnp.int32)[owner] - position) % ring_size
    block_queries = jnp.take(ring_queries, owner_offset, axis=0)
    keys_here = kv_cache[0].reshape(local_blocks, block_size, local_heads, HD)
    values_here = kv_cache[1].reshape(local_blocks, block_size, local_heads, HD)
    scores = (
        jnp.einsum(
            "bnkhc,bthc->bhnkt", block_queries, keys_here, preferred_element_type=jnp.float32
        )
        * scale_q
    )
    key_pos = ordinal[:, None] * block_size + jnp.arange(block_size, dtype=jnp.int32)[None, :]
    key_ok = key_pos < cached_len[owner][:, None]
    scores = jnp.where(key_ok[:, None, None, None, :], scores, NEG_FILL)
    block_best = jnp.max(scores, axis=-1)
    request_best = jnp.max(
        jnp.where(owns[:, :, None, None, None], block_best[None], NEG_FILL), axis=1
    )
    best_hi, best_lo = split_bf16(request_best)
    request_ref = best_hi + best_lo
    weights = jnp.exp(scores - jnp.take(request_ref, owner, axis=0)[..., None])
    block_totals = jnp.sum(weights, axis=-1)
    block_accum = jnp.einsum(
        "bhnkt,bthc->bhnkc",
        weights.astype(jnp.bfloat16),
        values_here,
        preferred_element_type=jnp.float32,
    )
    owns_f = owns.astype(jnp.float32)
    accum = jnp.einsum("rb,bhnkc->rhnkc", owns_f, block_accum, precision=lax.Precision.HIGHEST)
    totals = jnp.einsum("rb,bhnk->rhnk", owns_f, block_totals, precision=lax.Precision.HIGHEST)
    totals_hi, totals_lo = split_bf16(totals)
    stats = jnp.stack([best_hi, best_lo, totals_hi, totals_lo], axis=1).astype(jnp.bfloat16)
    stat_rows = stats.size // (request_count * HD)
    payload = jnp.concatenate(
        [
            accum.astype(jnp.bfloat16).reshape(request_count, -1, HD),
            stats.reshape(request_count, stat_rows, HD),
        ],
        axis=1,
    )
    received = lax.all_to_all(payload, "seq", 0, 0, tiled=True)
    acc_rows = local_heads * new_count * 2
    sources = received.shape[0]
    part_accum = (
        received[:, :acc_rows].astype(jnp.float32).reshape(sources, local_heads, new_count, 2, HD)
    )
    part_stats = (
        received[:, acc_rows:].astype(jnp.float32).reshape(sources, 4, local_heads, new_count, 2)
    )
    part_best = part_stats[:, 0] + part_stats[:, 1]
    part_totals = part_stats[:, 2] + part_stats[:, 3]
    cache_best = jnp.max(part_best, axis=0)
    factor = jnp.exp(part_best - cache_best[None])
    cache_total = jnp.sum(part_totals * factor, axis=0)
    cache_accum = jnp.sum(part_accum * factor[..., None], axis=0)
    peak = jnp.maximum(cache_best, self_best)
    cache_share = jnp.exp(cache_best - peak)
    self_share = jnp.exp(self_best - peak)
    numerator = cache_accum * cache_share[..., None] + self_accum * self_share[..., None]
    denominator = cache_total * cache_share + self_total * self_share
    attended = jnp.transpose(
        (numerator / denominator[..., None]).astype(jnp.bfloat16), (1, 2, 0, 3)
    ).reshape(new_count, 2, local_heads * HD)
    rows_each = new_count // head_count
    output = jnp.zeros((rows_each * lax.axis_size("heads"), o_weight.shape[2]), jnp.float32)
    for expert in range(o_weight.shape[0]):
        weight_expert = jnp.sum(onehot[:, :, expert] * gates, axis=1)
        picked = jnp.where(
            chosen[:, 0:1] == expert,
            attended[:, 0],
            jnp.where(chosen[:, 1:2] == expert, attended[:, 1], jnp.zeros_like(attended[:, 0])),
        )
        output = output + weight_expert[:, None] * jnp.dot(
            picked, o_weight[expert], preferred_element_type=jnp.float32
        )
    summed = shift_reduce_scatter(output.astype(jnp.bfloat16), "heads")
    return summed[None].astype(jnp.bfloat16)


def solution(mesh):
    return jax.shard_map(
        functools.partial(per_device, tuple(seq_cycle(mesh))),
        mesh=mesh,
        in_specs=(
            P("seq", "heads", None),
            P(),
            P(),
            P("seq", None, None),
            P(None, None, "heads"),
            P(None, None, "heads"),
            P(None, "heads", None),
            P(None, "seq", None, "heads"),
            P(),
            P(),
            P(),
        ),
        out_specs=P("seq", "heads", None),
        check_vma=False,
    )
```

profile of v0, /device:TPU:0, one launch (start us, length us, event | category | flops | bytes accessed | tf_op | source)
XLA Modules:
  0.0 194.5 jit_solution(13304430576117952579)
XLA Ops:
  6.5 0.8 convert_element_type.89
  7.4 1.1 fusion.36
  8.5 1.8 fusion.38
  10.3 0.8 reduce-window.9
  11.2 0.7 bitcast_subtract_fusion.1
  11.8 0.8 select_reduce_fusion.1
  12.8 0.7 gather_fusion
  13.4 0.7 gather_fusion.1
  14.1 0.7 dynamic_slice.19
  14.8 0.7 gather_fusion.2
  15.4 0.7 dynamic_slice.18
  16.1 0.7 add_convert_fusion.3
  16.8 2.7 %fusion.126 = (bf16[1,16,128,256]{3,2,1,0:T(8,128)(2,1)}, bf16[1,16,128,256]{3,2,1,0:T(8,128)(2,1)S(1)}) fusion(bf16[2,16,128,256]{3,2,1,0:T(8,128)(2,1)} %param.20), kind=kLoop, calls=%fused_computation.220 | loop fusion | bytes 4194304 | tf_op jit(solution)/shard_map/slice | solution.py:199
  19.6 1.3 copy.264
  20.9 0.7 fusion.114
  22.2 1.6 copy.265
  25.0 1.2 compare_and_fusion
  26.4 1.2 multiply_cosine_fusion
  27.5 2.4 %all-gather.2.cloned.1.call-done = bf16[256,2048]{1,0:T(8,128)(2,1)} async-done(((bf16[64,2048]{1,0:T(8,128)(2,1)}), bf16[256,2048]{1,0:T(8,128)(2,1)}) %all-gather.2.cloned.1.call-update) | async-done | bytes 1048592 | tf_op jit(solution)/shard_map/all_gather | solution.py:146
  29.9 3.8 %fusion.28 = f32[256,4,256]{2,0,1:T(8,128)S(1)} fusion(bf16[4,2048,256]{2,1,0:T(8,128)(2,1)} %param.17, bf16[256,2048]{1,0:T(8,128)(2,1)} %all-gather.2.cloned.1.call-done), kind=kOutput, calls=%fused_computation.41 | convolution fusion | flops 1073741824 | bytes 6291456 | tf_op jit(solution)/shard_map/nd,edc->nec/dot_general | solution.py:152
  33.7 1.1 multiply_reduce_fusion.1
  34.8 2.1 %copy.211 = f32[256,2,256]{0,2,1:T(8,128)} copy(f32[256,2,256]{2,0,1:T(8,128)} %multiply_reduce_fusion.1) | data formatting | bytes 1048576 | tf_op jit(solution)/shard_map/reduce_sum | solution.py:153
  36.9 1.8 fusion.127
  38.6 1.9 copy.261
  40.6 1.0 copy.260
  41.6 1.4 subtract_convert_fusion
  43.1 0.7 copy-done.4
  43.8 0.8 pad_maximum_fusion.1
  44.6 1.5 collective-permute-start
  46.6 1.0 convolution_bitcast_fusion
  47.7 0.7 copy-done.9
  48.6 1.0 subtract_convert_fusion.1
  49.6 1.0 slice.236
  50.6 1.4 fusion.129
  52.0 2.6 %collective-permute-done.3 = bf16[256,2,2,128]{3,0,1,2:T(8,128)(2,1)} collective-permute-done((bf16[256,2,2,128]{3,0,1,2:T(8,128)(2,1)}, bf16[256,2,2,128]{3,0,1,2:T(8,128)(2,1)}, u32[]{:S(2)}, u32[]{:S(2)}) %collective-permute-start.3) | collective-permute-done | bytes 262176 | tf_op jit(solution)/shard_map/ppermute | solution.py:116
  55.1 1.2 fusion.39
  56.3 1.5 collective-permute-start.1
  57.9 4.1 %collective-permute-done.4 = bf16[256,2,2,128]{3,0,1,2:T(8,128)(2,1)S(1)} collective-permute-done((bf16[256,2,2,128]{3,0,1,2:T(8,128)(2,1)}, bf16[256,2,2,128]{3,0,1,2:T(8,128)(2,1)S(1)}, u32[]{:S(2)}, u32[]{:S(2)}) %collective-permute-start.4) | collective-permute-done | bytes 262176 | tf_op jit(solution)/shard_map/ppermute | solution.py:116
  62.8 0.7 collective-permute-done.1
  63.5 1.5 collective-permute-start.2
  65.0 1.0 bitcast_dynamic-update-slice_fusion.6
  66.0 2.8 %collective-permute-done.5 = bf16[256,2,2,128]{3,0,1,2:T(8,128)(2,1)S(1)} collective-permute-done((bf16[256,2,2,128]{3,0,1,2:T(8,128)(2,1)S(1)}, bf16[256,2,2,128]{3,0,1,2:T(8,128)(2,1)S(1)}, u32[]{:S(2)}, u32[]{:S(2)}) %collective-permute-start.5) | collective-permute-done | bytes 262176 | tf_op jit(solution)/shard_map/ppermute | solution.py:116
  69.9 5.2 %collective-permute-done.6 = bf16[256,2,2,128]{3,0,1,2:T(8,128)(2,1)S(1)} collective-permute-done((bf16[256,2,2,128]{3,0,1,2:T(8,128)(2,1)S(1)}, bf16[256,2,2,128]{3,0,1,2:T(8,128)(2,1)S(1)}, u32[]{:S(2)}, u32[]{:S(2)}) %collective-permute-start.6) | collective-permute-done | bytes 262176 | tf_op jit(solution)/shard_map/ppermute | solution.py:116
  75.3 1.0 bitcast_dynamic-update-slice_fusion
  76.3 3.2 %gather_fusion.3 = bf16[16,256,2,2,128]{4,1,2,3,0:T(8,128)(2,1)} fusion(bf16[8,256,2,2,128]{4,1,2,3,0:T(8,128)(2,1)S(1)} %bitcast_dynamic-update-slice_fusion, s32[1024]{0:T(1024)} %pad_clamp_fusion), kind=kCustom, calls=%fused_computation.3 | custom fusion | bytes 8388672 | tf_op jit(solution)/shard_map/jit(_take)/gather | solution.py:197
  79.5 8.0 %fusion.2 = (f32[16,2,256,2]{2,3,1,0:T(2,128)S(1)}, f32[16,2,256,2,128]{2,4,3,1,0:T(8,128)}) fusion(pred[16,128]{1,0:T(8,128)(4,1)S(1)} %add_compare_fusion, bf16[16,128,2,128,1]{1,3,4,2,0:T(8,128)(2,1)} %bitcast.182, bf16[16,256,2,2,128]{4,1,2,3,0:T(8,128)(2,1)} %gather_fusion.3, pred[16]{0:T(512)(128)(4,1)S(1)} %copy-done.18), kind=kOutput, calls=%fused_computation.9 | convolution fusion | flops 545243136 | bytes 13699088 | tf_op jit(solution)/shard_map/bnkhc,bthc->bhnkt/dot_general | solution.py:201
  87.8 0.7 gather_fusion.4
  88.6 4.7 %fusion.3 = f32[16,2,256,2]{2,3,1,0:T(2,128)S(1)} fusion(f32[16,2,256,2,128]{2,4,3,1,0:T(8,128)} %get-tuple-element.54, f32[16,2,256,2]{2,3,1,0:T(2,128)S(1)} %broadcast_select_fusion, pred[16,128]{1,0:T(8,128)(4,1)S(1)} %add_compare_fusion), kind=kLoop, calls=%fused_computation.10 | loop fusion | flops 8372224 | bytes 8521728 | tf_op jit(solution)/shard_map/reduce_sum | solution.py:216
  93.5 0.7 copy.231
  94.6 5.2 %fusion.5 = f32[16,2,256,2,128]{4,2,3,1,0:T(8,128)S(1)} fusion(bf16[16,128,2,128,1]{1,3,4,2,0:T(8,128)(2,1)S(1)} %bitcast.172, f32[16,2,256,2,128]{2,4,3,1,0:T(8,128)} %get-tuple-element.54, f32[16,2,256,2]{2,3,1,0:T(2,128)S(1)} %broadcast_select_fusion, pred[16,128]{1,0:T(8,128)(4,1)S(1)} %add_compare_fusion), kind=kOutput, calls=%fused_computation.12 | convolution fusion | flops 545259520 | bytes 17893376 | tf_op jit(solution)/shard_map/bhnkt,bthc->bhnkc/dot_general | solution.py:217
  99.8 6.3 %fusion.19 = bf16[8,2,256,2,128]{4,0,3,2,1:T(8,128)(2,1)S(1)} fusion(f32[16,2,256,2,128]{4,2,3,1,0:T(8,128)S(1)} %fusion.5, s32[16]{0:T(128)S(1)} %copy-done.16), kind=kOutput, calls=%fused_computation.32 | convolution fusion | flops 202375296 | bytes 10485824 | tf_op jit(solution)/shard_map/rb,bhnkc->rhnkc/dot_general | solution.py:224
  106.4 1.5 pad_maximum_fusion
  107.9 4.7 %all-to-all-start = ((bf16[8,1056,128]{2,1,0:T(8,128)(2,1)}), bf16[8,1056,128]{2,1,0:T(8,128)(2,1)}, u32[]{:S(2)}, u32[]{:S(2)}) async-start(bf16[8,1056,128]{2,1,0:T(8,128)(2,1)} %pad_maximum_fusion), calls=%async_computation | async-start | bytes 4325376 | tf_op jit(solution)/shard_map/all_to_all | solution.py:236
  113.2 45.3 %all-to-all-done = bf16[8,1056,128]{2,1,0:T(8,128)(2,1)} async-done(((bf16[8,1056,128]{2,1,0:T(8,128)(2,1)}), bf16[8,1056,128]{2,1,0:T(8,128)(2,1)}, u32[]{:S(2)}, u32[]{:S(2)}) %all-to-all-start) | async-done | bytes 2162720 | tf_op jit(solution)/shard_map/all_to_all | solution.py:236
  158.5 0.9 slice_convert_fusion.1
  160.9 1.3 fusion.43
  162.6 3.1 %multiply_reduce_fusion = f32[1024,128]{1,0:T(8,128)S(1)} fusion(bf16[8,1056,128]{2,1,0:T(8,128)(2,1)} %all-to-all-done, f32[8,1024]{1,0:T(8,128)S(1)} %subtract_exponential_fusion.2), kind=kLoop, calls=%fused_computation.13 | loop fusion | flops 3014656 | bytes 2654208 | tf_op jit(solution)/shard_map/reduce_sum | solution.py:250
  166.4 1.7 convolution_multiply_fusion.3
  168.1 1.9 fusion.16
  171.5 0.9 constant_dynamic-slice_fusion.1
  172.9 6.5 %collective-permute-done.9 = bf16[64,2048]{1,0:T(8,128)(2,1)} collective-permute-done((bf16[64,2048]{1,0:T(8,128)(2,1)}, bf16[64,2048]{1,0:T(8,128)(2,1)}, u32[]{:S(2)}, u32[]{:S(2)}) %collective-permute-start.9) | collective-permute-done | bytes 262176 | tf_op jit(solution)/shard_map/ppermute | solution.py:102
  179.4 5.4 %collective-permute-done.8 = bf16[64,2048]{1,0:T(8,128)(2,1)} collective-permute-done((bf16[64,2048]{1,0:T(8,128)(2,1)}, bf16[64,2048]{1,0:T(8,128)(2,1)}, u32[]{:S(2)}, u32[]{:S(2)}) %collective-permute-start.8) | collective-permute-done | bytes 262176 | tf_op jit(solution)/shard_map/ppermute | solution.py:102
  184.9 0.8 collective-permute-done.7
  185.7 1.9 fusion.49
  (100 shorter events, 11.8 us)
Async XLA Ops:
  6.5 40.1 %copy-start = (bf16[2,2048,256]{2,1,0:T(8,128)(2,1)S(1)}, bf16[2,2048,256]{2,1,0:T(8,128)(2,1)}, u32[]{:S(2)}) copy-start(bf16[2,2048,256]{2,1,0:T(8,128)(2,1)} %param.18) | copy-start | bytes 6291460
  6.5 8.2 %copy-start.2 = (s32[8]{0:T(128)S(1)}, s32[8]{0:T(128)}, u32[]{:S(2)}) copy-start(s32[8]{0:T(128)} %constant.127.clone) | copy-start | bytes 100
  6.5 9.6 %copy-start.11 = (s32[1,256,2]{1,2,0:T(2,128)S(1)}, s32[1,256,2]{1,2,0:T(2,128)}, u32[]{:S(2)}) copy-start(s32[1,256,2]{1,2,0:T(2,128)} %param.16) | copy-start | bytes 6148
  6.5 23.4 %all-gather.2.cloned.1.call-start = ((), (), s32[]{:S(2)}) async-start(), calls=%async_computation.1 | async-start | bytes 1310720 | tf_op jit(solution)/shard_map/all_gather | solution.py:146
  12.8 3.4 %copy-start.13 = (s32[1024]{0:T(1024)}, s32[1024]{0:T(1024)S(1)}, u32[]{:S(2)}) copy-start(s32[1024]{0:T(1024)S(1)} %pad_clamp_fusion.1) | copy-start | bytes 12292
  24.4 9.2 %copy-start.15 = (s32[16]{0:T(128)}, s32[16]{0:T(128)S(1)}, u32[]{:S(2)}) copy-start(s32[16]{0:T(128)S(1)} %broadcast_add_fusion) | copy-start | bytes 196
  41.6 5.0 %copy-start.7 = (bf16[256,2048]{1,0:T(8,128)(2,1)S(1)}, bf16[256,2048]{1,0:T(8,128)(2,1)}, u32[]{:S(2)}) copy-start(bf16[256,2048]{1,0:T(8,128)(2,1)} %all-gather.2.cloned.1.call-done) | copy-start | bytes 3145732
  43.0 0.7 copy-start.4
  44.6 11.7 %collective-permute-start = (bf16[256,2,2,128]{3,0,1,2:T(8,128)(2,1)}, bf16[256,2,2,128]{3,0,1,2:T(8,128)(2,1)}, u32[]{:S(2)}, u32[]{:S(2)}) collective-permute-start(bf16[256,2,2,128]{3,0,1,2:T(8,128)(2,1)} %pad_maximum_fusion.1), channel_id=1, source_target_pairs={{1,0},{3,1},{5,3},{7,5},{6,7},{4,6},{2,4},{0,2},{9,8},{11,9},{13,1... | collective-permute-start | bytes 786440 | tf_op jit(solution)/shard_map/ppermute | solution.py:120
  46.1 8.5 %collective-permute-start.3 = (bf16[256,2,2,128]{3,0,1,2:T(8,128)(2,1)}, bf16[256,2,2,128]{3,0,1,2:T(8,128)(2,1)}, u32[]{:S(2)}, u32[]{:S(2)}) collective-permute-start(bf16[256,2,2,128]{3,0,1,2:T(8,128)(2,1)} %pad_maximum_fusion.1), channel_id=1, source_target_pairs={{0,1},{1,3},{3,5},{5,7},{7,6},{6,4},{4,2},{2,0},{8,9},{9,11},{11,1... | collective-permute-start | bytes 786440 | tf_op jit(solution)/shard_map/ppermute | solution.py:116
  47.6 0.8 copy-start.9
  47.6 3.0 %copy-start.10 = (pred[256,256]{0,1:T(8,128)(4,1)S(1)}, pred[256,256]{0,1:T(8,128)(4,1)}, u32[]{:S(2)}) copy-start(pred[256,256]{0,1:T(8,128)(4,1)} %iota_compare_fusion) | copy-start | bytes 196612
  50.6 12.0 %copy-start.5 = (bf16[256,2,2,64]{3,0,1,2:T(8,128)(2,1)S(1)}, bf16[256,2,2,64]{3,0,1,2:T(8,128)(2,1)}, u32[]{:S(2)}) copy-start(bf16[256,2,2,64]{3,0,1,2:T(8,128)(2,1)} %copy-done.4) | copy-start | bytes 393220
  54.6 7.5 %collective-permute-start.4 = (bf16[256,2,2,128]{3,0,1,2:T(8,128)(2,1)}, bf16[256,2,2,128]{3,0,1,2:T(8,128)(2,1)S(1)}, u32[]{:S(2)}, u32[]{:S(2)}) collective-permute-start(bf16[256,2,2,128]{3,0,1,2:T(8,128)(2,1)} %collective-permute-done.3), channel_id=1, source_target_pairs={{0,1},{1,3},{3,5},{5,7},{7,6},{6,4},{4,2},{2,0},{8,9},{9,11},{11,1... | collective-permute-start | bytes 786440 | tf_op jit(solution)/shard_map/ppermute | solution.py:116
  56.3 7.2 %collective-permute-start.1 = (bf16[256,2,2,128]{3,0,1,2:T(8,128)(2,1)}, bf16[256,2,2,128]{3,0,1,2:T(8,128)(2,1)S(1)}, u32[]{:S(2)}, u32[]{:S(2)}) collective-permute-start(bf16[256,2,2,128]{3,0,1,2:T(8,128)(2,1)} %collective-permute-done), channel_id=1, source_target_pairs={{1,0},{3,1},{5,3},{7,5},{6,7},{4,6},{2,4},{0,2},{9,8},{11,9},{13,1... | collective-permute-start | bytes 786440 | tf_op jit(solution)/shard_map/ppermute | solution.py:120
  62.1 6.7 %collective-permute-start.5 = (bf16[256,2,2,128]{3,0,1,2:T(8,128)(2,1)S(1)}, bf16[256,2,2,128]{3,0,1,2:T(8,128)(2,1)S(1)}, u32[]{:S(2)}, u32[]{:S(2)}) collective-permute-start(bf16[256,2,2,128]{3,0,1,2:T(8,128)(2,1)S(1)} %collective-permute-done.4), channel_id=1, source_target_pairs={{0,1},{1,3},{3,5},{5,7},{7,6},{6,4},{4,2},{2,0},{8,9},{9,11},{11,1... | collective-permute-start | bytes 786440 | tf_op jit(solution)/shard_map/ppermute | solution.py:116
  63.5 6.4 %collective-permute-start.2 = (bf16[256,2,2,128]{3,0,1,2:T(8,128)(2,1)S(1)}, bf16[256,2,2,128]{3,0,1,2:T(8,128)(2,1)S(1)}, u32[]{:S(2)}, u32[]{:S(2)}) collective-permute-start(bf16[256,2,2,128]{3,0,1,2:T(8,128)(2,1)S(1)} %collective-permute-done.1), channel_id=1, source_target_pairs={{1,0},{3,1},{5,3},{7,5},{6,7},{4,6},{2,4},{0,2},{9,8},{11,9},{13,1... | collective-permute-start | bytes 786440 | tf_op jit(solution)/shard_map/ppermute | solution.py:120
  68.8 6.4 %collective-permute-start.6 = (bf16[256,2,2,128]{3,0,1,2:T(8,128)(2,1)S(1)}, bf16[256,2,2,128]{3,0,1,2:T(8,128)(2,1)S(1)}, u32[]{:S(2)}, u32[]{:S(2)}) collective-permute-start(bf16[256,2,2,128]{3,0,1,2:T(8,128)(2,1)S(1)} %collective-permute-done.5), channel_id=1, source_target_pairs={{0,1},{1,3},{3,5},{5,7},{7,6},{6,4},{4,2},{2,0},{8,9},{9,11},{11,1... | collective-permute-start | bytes 786440 | tf_op jit(solution)/shard_map/ppermute | solution.py:116
  76.3 3.2 %copy-start.18 = (pred[16]{0:T(512)(128)(4,1)S(1)}, pred[16]{0:T(512)(128)(4,1)}, u32[]{:S(2)}) copy-start(pred[16]{0:T(512)(128)(4,1)} %get-tuple-element.56) | copy-start | bytes 52
  79.5 8.0 %copy-start.17 = (pred[8,16]{1,0:T(8,128)(4,1)S(1)}, pred[8,16]{1,0:T(8,128)(4,1)}, u32[]{:S(2)}) copy-start(pred[8,16]{1,0:T(8,128)(4,1)} %iota_compare_fusion.2) | copy-start | bytes 388
  87.8 0.8 copy-start.14
  88.6 4.7 %copy-start.16 = (s32[16]{0:T(128)S(1)}, s32[16]{0:T(128)}, u32[]{:S(2)}) copy-start(s32[16]{0:T(128)} %copy-done.15) | copy-start | bytes 196
  107.9 4.8 %copy-start.8 = (bf16[256,2048]{1,0:T(8,128)(2,1)S(1)}, bf16[256,2048]{1,0:T(8,128)(2,1)}, u32[]{:S(2)}) copy-start(bf16[256,2048]{1,0:T(8,128)(2,1)} %all-gather.2.cloned.1.call-done) | copy-start | bytes 3145732
  107.9 4.8 %copy-start.12 = (bf16[2048,4]{0,1:T(4,128)(2,1)S(1)}, bf16[2048,4]{0,1:T(4,128)(2,1)}, u32[]{:S(2)}) copy-start(bf16[2048,4]{0,1:T(4,128)(2,1)} %param.15) | copy-start | bytes 49156
  107.9 50.6 %all-to-all-start = ((bf16[8,1056,128]{2,1,0:T(8,128)(2,1)}), bf16[8,1056,128]{2,1,0:T(8,128)(2,1)}, u32[]{:S(2)}, u32[]{:S(2)}) async-start(bf16[8,1056,128]{2,1,0:T(8,128)(2,1)} %pad_maximum_fusion), calls=%async_computation | async-start | bytes 4325376 | tf_op jit(solution)/shard_map/all_to_all | solution.py:236
  162.2 3.5 %copy-start.6 = (f32[2,256,2,128]{3,1,2,0:T(8,128)S(1)}, f32[2,256,2,128]{3,1,2,0:T(8,128)}, u32[]{:S(2)}) copy-start(f32[2,256,2,128]{3,1,2,0:T(8,128)} %fusion.39) | copy-start | bytes 1572868
  168.1 2.5 %copy-start.3 = (bf16[4,256,2048]{2,1,0:T(8,128)(2,1)S(1)}, bf16[4,256,2048]{2,1,0:T(8,128)(2,1)}, u32[]{:S(2)}) copy-start(bf16[4,256,2048]{2,1,0:T(8,128)(2,1)} %param.19) | copy-start | bytes 12582916
  171.1 16.6 %copy-start.1 = (bf16[2,2048,256]{2,1,0:T(8,128)(2,1)S(1)}, bf16[2,2048,256]{2,1,0:T(8,128)(2,1)}, u32[]{:S(2)}) copy-start(bf16[2,2048,256]{2,1,0:T(8,128)(2,1)} %param.18) | copy-start | bytes 6291460
  172.4 7.0 %collective-permute-start.9 = (bf16[64,2048]{1,0:T(8,128)(2,1)}, bf16[64,2048]{1,0:T(8,128)(2,1)}, u32[]{:S(2)}, u32[]{:S(2)}) collective-permute-start(bf16[64,2048]{1,0:T(8,128)(2,1)} %get-tuple-element.35), channel_id=1, source_target_pairs={{0,24},{8,0},{16,8},{24,16},{1,25},{9,1},{17,9},{25,17},{2,26},{10... | collective-permute-start | bytes 786440 | tf_op jit(solution)/shard_map/ppermute | solution.py:102
  172.4 12.5 %collective-permute-start.8 = (bf16[64,2048]{1,0:T(8,128)(2,1)}, bf16[64,2048]{1,0:T(8,128)(2,1)}, u32[]{:S(2)}, u32[]{:S(2)}) collective-permute-start(bf16[64,2048]{1,0:T(8,128)(2,1)} %get-tuple-element.36), channel_id=1, source_target_pairs={{0,16},{8,24},{16,0},{24,8},{1,17},{9,25},{17,1},{25,9},{2,18},{10... | collective-permute-start | bytes 786440 | tf_op jit(solution)/shard_map/ppermute | solution.py:102
  172.6 13.1 %collective-permute-start.7 = (bf16[64,2048]{1,0:T(8,128)(2,1)S(1)}, bf16[64,2048]{1,0:T(8,128)(2,1)}, u32[]{:S(2)}, u32[]{:S(2)}) collective-permute-start(bf16[64,2048]{1,0:T(8,128)(2,1)S(1)} %get-tuple-element.34), channel_id=1, source_target_pairs={{0,8},{8,16},{16,24},{24,0},{1,9},{9,17},{17,25},{25,1},{2,10},{10... | collective-permute-start | bytes 786440 | tf_op jit(solution)/shard_map/ppermute | solution.py:102
Sparse Core Ops, SparseCore 0:
  10.4 19.4 all-gather.1
where the time goes:
time: 195 us; the launch traced here: 194 us
  waiting for transfers between devices  76.4 us (39%)
  matrix products  31.8 us (16%)
  other arithmetic  31.7 us (16%)
  local copies, waits for them, and re-layouts  28.7 us (15%)
  between operations  14 us (7%)
  starting transfers between devices  11.9 us (6%)
    all_to_all x1, waiting for transfers between devices, per_device(): received = lax.all_to_all(payload, 'seq', 0, 0, tiled=True)  45.3 us
    ppermute x4, waiting for transfers between devices, ring_all_gather(): moving = lax.ppermute(moving, axis_name, forward)  14.7 us
    ppermute x3, waiting for transfers between devices, shift_reduce_scatter(): lax.ppermute(piece, axis_name, [(i, (i + s) % size) for i in range(size)])  12.8 us
    unnamed x50, local copies, waits for them, and re-layouts  9.4 us
    dot_general x1, matrix products, per_device(): jnp.einsum('bnkhc,bthc->bhnkt', block_queries, keys_here, preferred_eleme...  7.99 us
    dot_general x1, matrix products, per_device(): jnp.einsum('rb,bhnkc->rhnkc', owns_f, block_accum, precision=lax.Precisio...  6.32 us
    dot_general x1, matrix products, per_device(): jnp.einsum('bhnkt,bthc->bhnkc', weights.astype(jnp.bfloat16), values_here...  5.22 us
    all_to_all x1, starting transfers between devices, per_device(): received = lax.all_to_all(payload, 'seq', 0, 0, tiled=True)  4.72 us
  transfers between devices with their start and end apart: 12, of which 11 were waited for; matrix products, arithmetic and copies ran while one was open for 13% of the time, Pallas kernels for 0%

commit v1 on v0

--- a/solution.py
+++ b/solution.py
@@ -233,7 +233,15 @@
         ],
         axis=1,
     )
-    received = lax.all_to_all(payload, "seq", 0, 0, tiled=True)
+    ways, here = (lax.axis_size("seq"), lax.axis_index("seq"))
+    width = payload.shape[0] // ways
+    turned = jnp.roll(payload, -here * width, axis=0)
+    got = [lax.slice_in_dim(turned, 0, width, axis=0)]
+    for far in range(1, ways):
+        sent = lax.slice_in_dim(turned, far * width, (far + 1) * width, axis=0)
+        got.append(lax.ppermute(sent, "seq", [(d_2, (d_2 + far) % ways) for d_2 in range(ways)]))
+    line_2 = jnp.concatenate(got[::-1], axis=0)
+    received = jnp.roll(line_2, (here + 1) * got[0].shape[0], axis=0)
     acc_rows = local_heads * new_count * 2
     sources = received.shape[0]
     part_accum = (

time: 195 us -> 197 us (1.010)
  waiting for transfers between devices: 76.4 us -> 53.8 us
  starting transfers between devices: 11.9 us -> 33.6 us
  other arithmetic: 31.7 us -> 35.1 us
  local copies, waits for them, and re-layouts: 28.7 us -> 25.7 us
    all_to_all x1 -> x0, waiting for transfers between devices: 45.3 us -> none  [per_device(): received = lax.all_to_all(payload, 'seq', 0, 0, tiled=True)]
    ppermute x0 -> x7, starting transfers between devices: none -> 24.2 us  [per_device(): lax.ppermute(sent, 'seq', [(d_2, (d_2 + far) % ways) for d_2 in range(way...]
    ppermute x0 -> x7, waiting for transfers between devices: none -> 22.8 us  [per_device(): lax.ppermute(sent, 'seq', [(d_2, (d_2 + far) % ways) for d_2 in range(way...]
    concatenate x1 -> x2, other arithmetic: 1.47 us -> 9.05 us  [the longest x1 8.27 us: per_device(): turned = jnp.roll(payload, -here * width, axis=0)]
    all_to_all x1 -> x0, starting transfers between devices: 4.72 us -> none  [per_device(): received = lax.all_to_all(payload, 'seq', 0, 0, tiled=True)]
    ppermute x4, starting transfers between devices: 2.16 us -> 5.87 us  [ring_all_gather(): moving = lax.ppermute(moving, axis_name, forward)]
    ppermute x3, starting transfers between devices: 4.46 us -> 1.77 us  [ring_all_gather(): moving = lax.ppermute(moving, axis_name, backward)]
    another operation x4, other arithmetic: 3.27 us -> 1.06 us
  transfers between devices with their start and end apart: 12 -> 18, of which waited for: 11 -> 10; matrix products, arithmetic and copies ran while one was open for 13% -> 12% of each run, Pallas kernels for 0% -> 0%
where the time goes in v1:
time: 197 us; the launch traced here: 196 us
  waiting for transfers between devices  53.8 us (27%)
  other arithmetic  35.1 us (18%)
  starting transfers between devices  33.6 us (17%)
  matrix products  33.6 us (17%)
  local copies, waits for them, and re-layouts  25.7 us (13%)
  between operations  14.3 us (7%)
    ppermute x7, starting transfers between devices, per_device(): lax.ppermute(sent, 'seq', [(d_2, (d_2 + far) % ways) for d_2 in range(way...  24.2 us
    ppermute x7, waiting for transfers between devices, per_device(): lax.ppermute(sent, 'seq', [(d_2, (d_2 + far) % ways) for d_2 in range(way...  22.8 us
    ppermute x4, waiting for transfers between devices, ring_all_gather(): moving = lax.ppermute(moving, axis_name, forward)  16.3 us
    ppermute x3, waiting for transfers between devices, shift_reduce_scatter(): lax.ppermute(piece, axis_name, [(i, (i + s) % size) for i in range(size)])  12.8 us
    unnamed x77, local copies, waits for them, and re-layouts  8.83 us
    concatenate x1, other arithmetic, per_device(): turned = jnp.roll(payload, -here * width, axis=0)  8.27 us
    dot_general x1, matrix products, per_device(): jnp.einsum('bnkhc,bthc->bhnkt', block_queries, keys_here, preferred_eleme...  7.99 us
    dot_general x1, matrix products, per_device(): jnp.einsum('rb,bhnkc->rhnkc', owns_f, block_accum, precision=lax.Precisio...  6.31 us
  transfers between devices with their start and end apart: 18, of which 10 were waited for; matrix products, arithmetic and copies ran while one was open for 12% of the time, Pallas kernels for 0%

profile of v1, /device:TPU:0, one launch (start us, length us, event | category | flops | bytes accessed | tf_op | source)
XLA Modules:
  0.0 196.0 jit_solution(13481133562619845250)
XLA Ops:
  6.5 1.3 fusion.40
  7.8 0.7 convert_element_type.89
  8.5 1.8 fusion.42
  10.4 0.8 reduce-window.9
  11.2 0.8 select_reduce_fusion.1
  12.1 0.7 bitcast_subtract_fusion.1
  12.9 0.7 gather_fusion
  13.5 0.7 gather_fusion.1
  14.2 0.7 dynamic_slice.22
  15.4 0.7 gather_fusion.2
  18.6 2.8 %fusion.131 = (bf16[1,16,128,256]{3,2,1,0:T(8,128)(2,1)S(1)}, bf16[1,16,128,256]{3,2,1,0:T(8,128)(2,1)}) fusion(bf16[2,16,128,256]{3,2,1,0:T(8,128)(2,1)} %param.22), kind=kLoop, calls=%fused_computation.238 | loop fusion | bytes 4194304 | tf_op jit(solution)/shard_map/slice | solution.py:198
  21.4 1.4 copy.264
  22.8 1.6 copy.265
  24.4 0.6 iota_compare_fusion
  25.7 1.2 compare_and_fusion
  27.0 1.2 multiply_cosine_fusion
  28.1 1.8 all-gather.2.cloned.1.call-done
  30.0 2.2 %convolution_bitcast_fusion = f32[2,256,256]{1,2,0:T(8,128)S(1)} fusion(bf16[2,2048,256]{2,1,0:T(8,128)(2,1)S(1)} %copy-done, bf16[256,2048]{1,0:T(8,128)(2,1)} %all-gather.2.cloned.1.call-done), kind=kOutput, calls=%fused_computation.44 | convolution fusion | flops 536870912 | bytes 3670016 | tf_op jit(solution)/shard_map/nd,sdc->snc/dot_general | solution.py:157
  32.2 0.7 slice.277
  32.9 3.5 %fusion.32 = f32[256,4,256]{2,0,1:T(8,128)S(1)} fusion(bf16[4,2048,256]{2,1,0:T(8,128)(2,1)} %param.19, bf16[256,2048]{1,0:T(8,128)(2,1)S(1)} %copy-done.10), kind=kOutput, calls=%fused_computation.50 | convolution fusion | flops 1073741824 | bytes 6291456 | tf_op jit(solution)/shard_map/nd,edc->nec/dot_general | solution.py:152
  38.0 1.5 collective-permute-start.3
  40.4 1.3 fusion.134
  41.7 2.1 %fusion.43 = f32[2,256,2,128]{3,1,2,0:T(8,128)} fusion(bf16[256,2,128,1]{0,2,3,1:T(8,128)(2,1)} %bitcast.184, f32[2,256,2,256]{1,3,2,0:T(8,128)S(1)} %get-tuple-element.60, f32[2,256,2]{1,2,0:T(2,128)S(1)} %get-tuple-element.11), kind=kOutput, calls=%fused_computation.64 | convolution fusion | flops 67633152 | bytes 1708032 | tf_op jit(solution)/shard_map/hnkt,thc->hnkc/dot_general | solution.py:187
  43.8 2.7 %collective-permute-done.3 = bf16[256,2,2,128]{3,0,1,2:T(8,128)(2,1)} collective-permute-done((bf16[256,2,2,128]{3,0,1,2:T(8,128)(2,1)S(1)}, bf16[256,2,2,128]{3,0,1,2:T(8,128)(2,1)}, u32[]{:S(2)}, u32[]{:S(2)}) %collective-permute-start.3) | collective-permute-done | bytes 262176 | tf_op jit(solution)/shard_map/ppermute | solution.py:116
  46.6 1.5 collective-permute-start.4
  49.2 5.3 %collective-permute-done.4 = bf16[256,2,2,128]{3,0,1,2:T(8,128)(2,1)S(1)} collective-permute-done((bf16[256,2,2,128]{3,0,1,2:T(8,128)(2,1)}, bf16[256,2,2,128]{3,0,1,2:T(8,128)(2,1)S(1)}, u32[]{:S(2)}, u32[]{:S(2)}) %collective-permute-start.4) | collective-permute-done | bytes 262176 | tf_op jit(solution)/shard_map/ppermute | solution.py:116
  54.4 1.4 collective-permute-start.5
  56.0 0.6 collective-permute-start.2
  56.7 1.0 bitcast_dynamic-update-slice_fusion.6
  57.7 3.5 %collective-permute-done.5 = bf16[256,2,2,128]{3,0,1,2:T(8,128)(2,1)S(1)} collective-permute-done((bf16[256,2,2,128]{3,0,1,2:T(8,128)(2,1)S(1)}, bf16[256,2,2,128]{3,0,1,2:T(8,128)(2,1)S(1)}, u32[]{:S(2)}, u32[]{:S(2)}) %collective-permute-start.5) | collective-permute-done | bytes 262176 | tf_op jit(solution)/shard_map/ppermute | solution.py:116
  61.1 1.4 collective-permute-start.6
  62.7 4.8 %collective-permute-done.6 = bf16[256,2,2,128]{3,0,1,2:T(8,128)(2,1)S(1)} collective-permute-done((bf16[256,2,2,128]{3,0,1,2:T(8,128)(2,1)S(1)}, bf16[256,2,2,128]{3,0,1,2:T(8,128)(2,1)S(1)}, u32[]{:S(2)}, u32[]{:S(2)}) %collective-permute-start.6) | collective-permute-done | bytes 262176 | tf_op jit(solution)/shard_map/ppermute | solution.py:116
  67.6 1.0 bitcast_dynamic-update-slice_fusion
  68.6 3.2 %gather_fusion.3 = bf16[16,256,2,2,128]{4,1,2,3,0:T(8,128)(2,1)} fusion(bf16[8,256,2,2,128]{4,1,2,3,0:T(8,128)(2,1)S(1)} %bitcast_dynamic-update-slice_fusion, s32[1024]{0:T(1024)} %pad_clamp_fusion), kind=kCustom, calls=%fused_computation.3 | custom fusion | bytes 8388672 | tf_op jit(solution)/shard_map/jit(_take)/gather | solution.py:197
  71.8 8.0 %fusion.2 = (f32[16,2,256,2]{2,3,1,0:T(2,128)S(1)}, f32[16,2,256,2,128]{2,4,3,1,0:T(8,128)}) fusion(pred[16,128]{1,0:T(8,128)(4,1)S(1)} %add_compare_fusion, bf16[16,128,2,128,1]{1,3,4,2,0:T(8,128)(2,1)} %bitcast.182, bf16[16,256,2,2,128]{4,1,2,3,0:T(8,128)(2,1)} %gather_fusion.3, pred[16]{0:T(512)(128)(4,1)S(1)} %copy-done.28), kind=kOutput, calls=%fused_computation.9 | convolution fusion | flops 545243136 | bytes 13699088 | tf_op jit(solution)/shard_map/bnkhc,bthc->bhnkt/dot_general | solution.py:201
  80.1 0.7 gather_fusion.4
  81.0 4.7 %fusion.3 = f32[16,2,256,2]{2,3,1,0:T(2,128)S(1)} fusion(f32[16,2,256,2,128]{2,4,3,1,0:T(8,128)} %get-tuple-element.62, f32[16,2,256,2]{2,3,1,0:T(2,128)S(1)} %broadcast_select_fusion, pred[16,128]{1,0:T(8,128)(4,1)S(1)} %add_compare_fusion), kind=kLoop, calls=%fused_computation.10 | loop fusion | flops 8372224 | bytes 8521728 | tf_op jit(solution)/shard_map/reduce_sum | solution.py:216
  85.7 5.2 %fusion.5 = f32[16,2,256,2,128]{4,2,3,1,0:T(8,128)S(1)} fusion(bf16[16,128,2,128,1]{1,3,4,2,0:T(8,128)(2,1)S(1)} %bitcast.172, f32[16,2,256,2,128]{2,4,3,1,0:T(8,128)} %get-tuple-element.62, f32[16,2,256,2]{2,3,1,0:T(2,128)S(1)} %broadcast_select_fusion, pred[16,128]{1,0:T(8,128)(4,1)S(1)} %add_compare_fusion), kind=kOutput, calls=%fused_computation.18 | convolution fusion | flops 545259520 | bytes 17893376 | tf_op jit(solution)/shard_map/bhnkt,bthc->bhnkc/dot_general | solution.py:217
  90.9 6.3 %fusion.23 = bf16[8,2,256,2,128]{4,0,3,2,1:T(8,128)(2,1)S(1)} fusion(f32[16,2,256,2,128]{4,2,3,1,0:T(8,128)S(1)} %fusion.5, s32[16]{0:T(128)S(1)} %copy-done.26), kind=kOutput, calls=%fused_computation.41 | convolution fusion | flops 202375296 | bytes 10485824 | tf_op jit(solution)/shard_map/rb,bhnkc->rhnkc/dot_general | solution.py:224
  97.7 1.0 copy.231
  99.0 8.3 %fusion.20 = bf16[8,1056,128]{2,1,0:T(8,128)(2,1)S(1)} fusion(s32[]{:T(128)S(6)} %select_n.195, bf16[8,1024,128]{2,1,0:T(8,128)(2,1)S(1)} %copy.232, bf16[8,32,128]{2,1,0:T(8,128)(2,1)S(1)} %copy.233), kind=kLoop, calls=%fused_computation.37 | loop fusion | flops 8650752 | bytes 4325380 | tf_op jit(solution)/shard_map/jit(_roll_dynamic)/concatenate | solution.py:238
  107.3 1.3 copy-done.3
  108.8 4.2 %collective-permute-start.7 = (bf16[1,1056,128]{2,1,0:T(8,128)(2,1)S(1)}, bf16[1,1056,128]{2,1,0:T(8,128)(2,1)S(1)}, u32[]{:S(2)}, u32[]{:S(2)}) collective-permute-start(bf16[1,1056,128]{2,1,0:T(8,128)(2,1)S(1)} %get-tuple-element.37), channel_id=1, source_target_pairs={{0,7},{1,0},{2,1},{3,2},{4,3},{5,4},{6,5},{7,6},{8,15},{9,8},{10,9... | collective-permute-start | bytes 811016 | tf_op jit(solution)/shard_map/ppermute | solution.py:242
  113.7 0.6 collective-permute-start.13
  114.3 0.9 collective-permute-start.12
  115.3 1.1 collective-permute-start.11
  116.4 3.6 %collective-permute-done.7 = bf16[1,1056,128]{2,1,0:T(8,128)(2,1)S(1)} collective-permute-done((bf16[1,1056,128]{2,1,0:T(8,128)(2,1)S(1)}, bf16[1,1056,128]{2,1,0:T(8,128)(2,1)S(1)}, u32[]{:S(2)}, u32[]{:S(2)}) %collective-permute-start.7) | collective-permute-done | bytes 270368 | tf_op jit(solution)/shard_map/ppermute | solution.py:242
  119.9 2.5 %collective-permute-start.9 = (bf16[1,1056,128]{2,1,0:T(8,128)(2,1)S(1)}, bf16[1,1056,128]{2,1,0:T(8,128)(2,1)S(1)}, u32[]{:S(2)}, u32[]{:S(2)}) collective-permute-start(bf16[1,1056,128]{2,1,0:T(8,128)(2,1)S(1)} %get-tuple-element.35), channel_id=1, source_target_pairs={{0,5},{1,6},{2,7},{3,0},{4,1},{5,2},{6,3},{7,4},{8,13},{9,14},{10,... | collective-permute-start | bytes 811016 | tf_op jit(solution)/shard_map/ppermute | solution.py:242
  122.4 9.0 %collective-permute-done.8 = bf16[1,1056,128]{2,1,0:T(8,128)(2,1)S(1)} collective-permute-done((bf16[1,1056,128]{2,1,0:T(8,128)(2,1)S(1)}, bf16[1,1056,128]{2,1,0:T(8,128)(2,1)S(1)}, u32[]{:S(2)}, u32[]{:S(2)}) %collective-permute-start.8) | collective-permute-done | bytes 270368 | tf_op jit(solution)/shard_map/ppermute | solution.py:242
  131.4 14.2 %collective-permute-start.10 = (bf16[1,1056,128]{2,1,0:T(8,128)(2,1)S(1)}, bf16[1,1056,128]{2,1,0:T(8,128)(2,1)S(1)}, u32[]{:S(2)}, u32[]{:S(2)}) collective-permute-start(bf16[1,1056,128]{2,1,0:T(8,128)(2,1)S(1)} %get-tuple-element.34), channel_id=1, source_target_pairs={{0,4},{1,5},{2,6},{3,7},{4,0},{5,1},{6,2},{7,3},{8,12},{9,13},{10,... | collective-permute-start | bytes 811016 | tf_op jit(solution)/shard_map/ppermute | solution.py:242
  145.8 10.2 %collective-permute-done.10 = bf16[1,1056,128]{2,1,0:T(8,128)(2,1)S(1)} collective-permute-done((bf16[1,1056,128]{2,1,0:T(8,128)(2,1)S(1)}, bf16[1,1056,128]{2,1,0:T(8,128)(2,1)S(1)}, u32[]{:S(2)}, u32[]{:S(2)}) %collective-permute-start.10) | collective-permute-done | bytes 270368 | tf_op jit(solution)/shard_map/ppermute | solution.py:242
  156.2 1.0 slice_dynamic-update-slice_fusion
  157.2 0.8 fusion.18
  158.0 1.3 copy-done.4
  160.0 0.6 fusion.129
  160.9 1.3 fusion.47
  162.6 3.1 %multiply_reduce_fusion = f32[1024,128]{1,0:T(8,128)S(1)} fusion(bf16[8,1056,128]{2,1,0:T(8,128)(2,1)} %copy-done.4, f32[8,1024]{1,0:T(8,128)S(1)} %subtract_exponential_fusion.2), kind=kLoop, calls=%fused_computation.19 | loop fusion | flops 3014656 | bytes 2654208 | tf_op jit(solution)/shard_map/reduce_sum | solution.py:258
  166.4 1.7 convolution_multiply_fusion.3
  168.2 1.9 fusion.16
  171.8 0.9 constant_dynamic-slice_fusion.2
  172.7 1.7 collective-permute-start.16
  174.4 7.1 %collective-permute-done.14 = bf16[64,2048]{1,0:T(8,128)(2,1)} collective-permute-done((bf16[64,2048]{1,0:T(8,128)(2,1)}, bf16[64,2048]{1,0:T(8,128)(2,1)}, u32[]{:S(2)}, u32[]{:S(2)}) %collective-permute-start.14) | collective-permute-done | bytes 262176 | tf_op jit(solution)/shard_map/ppermute | solution.py:102
  181.5 5.7 %collective-permute-done.15 = bf16[64,2048]{1,0:T(8,128)(2,1)} collective-permute-done((bf16[64,2048]{1,0:T(8,128)(2,1)S(1)}, bf16[64,2048]{1,0:T(8,128)(2,1)}, u32[]{:S(2)}, u32[]{:S(2)}) %collective-permute-start.15) | collective-permute-done | bytes 262176 | tf_op jit(solution)/shard_map/ppermute | solution.py:102
  187.2 1.9 fusion.53
  (143 shorter events, 13.6 us)
Async XLA Ops:
  6.5 23.4 %copy-start = (bf16[2,2048,256]{2,1,0:T(8,128)(2,1)S(1)}, bf16[2,2048,256]{2,1,0:T(8,128)(2,1)}, u32[]{:S(2)}) copy-start(bf16[2,2048,256]{2,1,0:T(8,128)(2,1)} %param.20) | copy-start | bytes 6291460
  6.5 8.3 %copy-start.2 = (s32[8]{0:T(128)S(1)}, s32[8]{0:T(128)}, u32[]{:S(2)}) copy-start(s32[8]{0:T(128)} %constant.144.clone) | copy-start | bytes 100
  6.5 9.6 %copy-start.13 = (s32[1,256,2]{1,2,0:T(2,128)S(1)}, s32[1,256,2]{1,2,0:T(2,128)}, u32[]{:S(2)}) copy-start(s32[1,256,2]{1,2,0:T(2,128)} %param.18) | copy-start | bytes 6148
  6.5 23.4 %all-gather.2.cloned.1.call-start = ((), (), s32[]{:S(2)}) async-start(), calls=%async_computation | async-start | bytes 1310720 | tf_op jit(solution)/shard_map/all_gather | solution.py:146
  12.8 5.7 %copy-start.15 = (s32[1024]{0:T(1024)}, s32[1024]{0:T(1024)S(1)}, u32[]{:S(2)}) copy-start(s32[1024]{0:T(1024)S(1)} %pad_clamp_fusion.1) | copy-start | bytes 12292
  25.1 7.9 %copy-start.25 = (s32[16]{0:T(128)}, s32[16]{0:T(128)S(1)}, u32[]{:S(2)}) copy-start(s32[16]{0:T(128)S(1)} %broadcast_add_fusion) | copy-start | bytes 196
  30.0 3.0 %copy-start.10 = (bf16[256,2048]{1,0:T(8,128)(2,1)S(1)}, bf16[256,2048]{1,0:T(8,128)(2,1)}, u32[]{:S(2)}) copy-start(bf16[256,2048]{1,0:T(8,128)(2,1)} %all-gather.2.cloned.1.call-done) | copy-start | bytes 3145732
  32.2 4.2 %copy-start.12 = (f32[2,256,256]{1,2,0:T(8,128)}, f32[2,256,256]{1,2,0:T(8,128)S(1)}, u32[]{:S(2)}) copy-start(f32[2,256,256]{1,2,0:T(8,128)S(1)} %convolution_bitcast_fusion) | copy-start | bytes 1572868
  36.8 0.9 copy-start.9
  37.0 3.0 %slice-start = ((f32[2,256,256]{1,2,0:T(8,128)}), f32[1,256,256]{1,2,0:T(8,128)S(1)}, s32[]{:S(2)}) async-start(f32[2,256,256]{1,2,0:T(8,128)} %copy-done.12), calls=%async_computation.1 | async-start | bytes 524288 | tf_op jit(solution)/shard_map/slice | solution.py:158
  37.8 3.9 %copy-start.6 = (bf16[256,2,2,64]{3,0,1,2:T(8,128)(2,1)}, bf16[256,2,2,64]{3,0,1,2:T(8,128)(2,1)S(1)}, u32[]{:S(2)}) copy-start(bf16[256,2,2,64]{3,0,1,2:T(8,128)(2,1)S(1)} %get-tuple-element.41) | copy-start | bytes 393220
  38.0 8.6 %collective-permute-start.3 = (bf16[256,2,2,128]{3,0,1,2:T(8,128)(2,1)S(1)}, bf16[256,2,2,128]{3,0,1,2:T(8,128)(2,1)}, u32[]{:S(2)}, u32[]{:S(2)}) collective-permute-start(bf16[256,2,2,128]{3,0,1,2:T(8,128)(2,1)S(1)} %pad_maximum_fusion), channel_id=1, source_target_pairs={{0,1},{1,3},{3,5},{5,7},{7,6},{6,4},{4,2},{2,0},{8,9},{9,11},{11,1... | collective-permute-start | bytes 786440 | tf_op jit(solution)/shard_map/ppermute | solution.py:116
  39.5 8.9 %collective-permute-start = (bf16[256,2,2,128]{3,0,1,2:T(8,128)(2,1)S(1)}, bf16[256,2,2,128]{3,0,1,2:T(8,128)(2,1)}, u32[]{:S(2)}, u32[]{:S(2)}) collective-permute-start(bf16[256,2,2,128]{3,0,1,2:T(8,128)(2,1)S(1)} %pad_maximum_fusion), channel_id=1, source_target_pairs={{1,0},{3,1},{5,3},{7,5},{6,7},{4,6},{2,4},{0,2},{9,8},{11,9},{13,1... | collective-permute-start | bytes 786440 | tf_op jit(solution)/shard_map/ppermute | solution.py:120
  40.3 7.7 %copy-start.11 = (bf16[256,2048]{1,0:T(8,128)(2,1)S(1)}, bf16[256,2048]{1,0:T(8,128)(2,1)}, u32[]{:S(2)}) copy-start(bf16[256,2048]{1,0:T(8,128)(2,1)} %all-gather.2.cloned.1.call-done) | copy-start | bytes 3145732
  40.4 7.7 %copy-start.14 = (bf16[2048,4]{0,1:T(4,128)(2,1)S(1)}, bf16[2048,4]{0,1:T(4,128)(2,1)}, u32[]{:S(2)}) copy-start(bf16[2048,4]{0,1:T(4,128)(2,1)} %param.17) | copy-start | bytes 49156
  41.7 14.1 %copy-start.7 = (bf16[256,2,2,64]{3,0,1,2:T(8,128)(2,1)S(1)}, bf16[256,2,2,64]{3,0,1,2:T(8,128)(2,1)}, u32[]{:S(2)}) copy-start(bf16[256,2,2,64]{3,0,1,2:T(8,128)(2,1)} %copy-done.6) | copy-start | bytes 393220
  46.6 7.8 %collective-permute-start.4 = (bf16[256,2,2,128]{3,0,1,2:T(8,128)(2,1)}, bf16[256,2,2,128]{3,0,1,2:T(8,128)(2,1)S(1)}, u32[]{:S(2)}, u32[]{:S(2)}) collective-permute-start(bf16[256,2,2,128]{3,0,1,2:T(8,128)(2,1)} %collective-permute-done.3), channel_id=1, source_target_pairs={{0,1},{1,3},{3,5},{5,7},{7,6},{6,4},{4,2},{2,0},{8,9},{9,11},{11,1... | collective-permute-start | bytes 786440 | tf_op jit(solution)/shard_map/ppermute | solution.py:116
  48.4 7.6 %collective-permute-start.1 = (bf16[256,2,2,128]{3,0,1,2:T(8,128)(2,1)}, bf16[256,2,2,128]{3,0,1,2:T(8,128)(2,1)S(1)}, u32[]{:S(2)}, u32[]{:S(2)}) collective-permute-start(bf16[256,2,2,128]{3,0,1,2:T(8,128)(2,1)} %collective-permute-done), channel_id=1, source_target_pairs={{1,0},{3,1},{5,3},{7,5},{6,7},{4,6},{2,4},{0,2},{9,8},{11,9},{13,1... | collective-permute-start | bytes 786440 | tf_op jit(solution)/shard_map/ppermute | solution.py:120
  54.4 6.7 %collective-permute-start.5 = (bf16[256,2,2,128]{3,0,1,2:T(8,128)(2,1)S(1)}, bf16[256,2,2,128]{3,0,1,2:T(8,128)(2,1)S(1)}, u32[]{:S(2)}, u32[]{:S(2)}) collective-permute-start(bf16[256,2,2,128]{3,0,1,2:T(8,128)(2,1)S(1)} %collective-permute-done.4), channel_id=1, source_target_pairs={{0,1},{1,3},{3,5},{5,7},{7,6},{6,4},{4,2},{2,0},{8,9},{9,11},{11,1... | collective-permute-start | bytes 786440 | tf_op jit(solution)/shard_map/ppermute | solution.py:116
  56.0 6.6 %collective-permute-start.2 = (bf16[256,2,2,128]{3,0,1,2:T(8,128)(2,1)S(1)}, bf16[256,2,2,128]{3,0,1,2:T(8,128)(2,1)S(1)}, u32[]{:S(2)}, u32[]{:S(2)}) collective-permute-start(bf16[256,2,2,128]{3,0,1,2:T(8,128)(2,1)S(1)} %collective-permute-done.1), channel_id=1, source_target_pairs={{1,0},{3,1},{5,3},{7,5},{6,7},{4,6},{2,4},{0,2},{9,8},{11,9},{13,1... | collective-permute-start | bytes 786440 | tf_op jit(solution)/shard_map/ppermute | solution.py:120
  61.1 6.4 %collective-permute-start.6 = (bf16[256,2,2,128]{3,0,1,2:T(8,128)(2,1)S(1)}, bf16[256,2,2,128]{3,0,1,2:T(8,128)(2,1)S(1)}, u32[]{:S(2)}, u32[]{:S(2)}) collective-permute-start(bf16[256,2,2,128]{3,0,1,2:T(8,128)(2,1)S(1)} %collective-permute-done.5), channel_id=1, source_target_pairs={{0,1},{1,3},{3,5},{5,7},{7,6},{6,4},{4,2},{2,0},{8,9},{9,11},{11,1... | collective-permute-start | bytes 786440 | tf_op jit(solution)/shard_map/ppermute | solution.py:116
  68.6 3.2 %copy-start.28 = (pred[16]{0:T(512)(128)(4,1)S(1)}, pred[16]{0:T(512)(128)(4,1)}, u32[]{:S(2)}) copy-start(pred[16]{0:T(512)(128)(4,1)} %get-tuple-element.64) | copy-start | bytes 52
  71.8 8.0 %copy-start.27 = (pred[8,16]{1,0:T(8,128)(4,1)S(1)}, pred[8,16]{1,0:T(8,128)(4,1)}, u32[]{:S(2)}) copy-start(pred[8,16]{1,0:T(8,128)(4,1)} %iota_compare_fusion.2) | copy-start | bytes 388
  80.1 0.8 copy-start.20
  85.7 5.2 %copy-start.26 = (s32[16]{0:T(128)S(1)}, s32[16]{0:T(128)}, u32[]{:S(2)}) copy-start(s32[16]{0:T(128)} %copy-done.25) | copy-start | bytes 196
  107.3 1.4 copy-start.3
  108.8 11.2 %collective-permute-start.7 = (bf16[1,1056,128]{2,1,0:T(8,128)(2,1)S(1)}, bf16[1,1056,128]{2,1,0:T(8,128)(2,1)S(1)}, u32[]{:S(2)}, u32[]{:S(2)}) collective-permute-start(bf16[1,1056,128]{2,1,0:T(8,128)(2,1)S(1)} %get-tuple-element.37), channel_id=1, source_target_pairs={{0,7},{1,0},{2,1},{3,2},{4,3},{5,4},{6,5},{7,6},{8,15},{9,8},{10,9... | collective-permute-start | bytes 811016 | tf_op jit(solution)/shard_map/ppermute | solution.py:242
  113.1 18.4 %collective-permute-start.8 = (bf16[1,1056,128]{2,1,0:T(8,128)(2,1)S(1)}, bf16[1,1056,128]{2,1,0:T(8,128)(2,1)S(1)}, u32[]{:S(2)}, u32[]{:S(2)}) collective-permute-start(bf16[1,1056,128]{2,1,0:T(8,128)(2,1)S(1)} %get-tuple-element.36), channel_id=1, source_target_pairs={{0,6},{1,7},{2,0},{3,1},{4,2},{5,3},{6,4},{7,5},{8,14},{9,15},{10,... | collective-permute-start | bytes 811016 | tf_op jit(solution)/shard_map/ppermute | solution.py:242
  113.7 42.5 %collective-permute-start.13 = (bf16[1,1056,128]{2,1,0:T(8,128)(2,1)S(1)}, bf16[1,1056,128]{2,1,0:T(8,128)(2,1)S(1)}, u32[]{:S(2)}, u32[]{:S(2)}) collective-permute-start(bf16[1,1056,128]{2,1,0:T(8,128)(2,1)S(1)} %get-tuple-element.31), channel_id=1, source_target_pairs={{0,1},{1,2},{2,3},{3,4},{4,5},{5,6},{6,7},{7,0},{8,9},{9,10},{10,1... | collective-permute-start | bytes 811016 | tf_op jit(solution)/shard_map/ppermute | solution.py:242
  114.3 41.8 %collective-permute-start.12 = (bf16[1,1056,128]{2,1,0:T(8,128)(2,1)S(1)}, bf16[1,1056,128]{2,1,0:T(8,128)(2,1)S(1)}, u32[]{:S(2)}, u32[]{:S(2)}) collective-permute-start(bf16[1,1056,128]{2,1,0:T(8,128)(2,1)S(1)} %get-tuple-element.32), channel_id=1, source_target_pairs={{0,2},{1,3},{2,4},{3,5},{4,6},{5,7},{6,0},{7,1},{8,10},{9,11},{10,... | collective-permute-start | bytes 811016 | tf_op jit(solution)/shard_map/ppermute | solution.py:242
  115.3 40.8 %collective-permute-start.11 = (bf16[1,1056,128]{2,1,0:T(8,128)(2,1)S(1)}, bf16[1,1056,128]{2,1,0:T(8,128)(2,1)S(1)}, u32[]{:S(2)}, u32[]{:S(2)}) collective-permute-start(bf16[1,1056,128]{2,1,0:T(8,128)(2,1)S(1)} %get-tuple-element.33), channel_id=1, source_target_pairs={{0,3},{1,4},{2,5},{3,6},{4,7},{5,0},{6,1},{7,2},{8,11},{9,12},{10,... | collective-permute-start | bytes 811016 | tf_op jit(solution)/shard_map/ppermute | solution.py:242
  119.9 25.8 %collective-permute-start.9 = (bf16[1,1056,128]{2,1,0:T(8,128)(2,1)S(1)}, bf16[1,1056,128]{2,1,0:T(8,128)(2,1)S(1)}, u32[]{:S(2)}, u32[]{:S(2)}) collective-permute-start(bf16[1,1056,128]{2,1,0:T(8,128)(2,1)S(1)} %get-tuple-element.35), channel_id=1, source_target_pairs={{0,5},{1,6},{2,7},{3,0},{4,1},{5,2},{6,3},{7,4},{8,13},{9,14},{10,... | collective-permute-start | bytes 811016 | tf_op jit(solution)/shard_map/ppermute | solution.py:242
  131.4 24.6 %collective-permute-start.10 = (bf16[1,1056,128]{2,1,0:T(8,128)(2,1)S(1)}, bf16[1,1056,128]{2,1,0:T(8,128)(2,1)S(1)}, u32[]{:S(2)}, u32[]{:S(2)}) collective-permute-start(bf16[1,1056,128]{2,1,0:T(8,128)(2,1)S(1)} %get-tuple-element.34), channel_id=1, source_target_pairs={{0,4},{1,5},{2,6},{3,7},{4,0},{5,1},{6,2},{7,3},{8,12},{9,13},{10,... | collective-permute-start | bytes 811016 | tf_op jit(solution)/shard_map/ppermute | solution.py:242
  158.0 1.4 copy-start.4
  162.2 3.5 %copy-start.8 = (f32[2,256,2,128]{3,1,2,0:T(8,128)S(1)}, f32[2,256,2,128]{3,1,2,0:T(8,128)}, u32[]{:S(2)}) copy-start(f32[2,256,2,128]{3,1,2,0:T(8,128)} %fusion.43) | copy-start | bytes 1572868
  162.6 3.9 %copy-start.21 = (pred[256]{0:T(512)(128)(4,1)S(1)}, pred[256]{0:T(512)(128)(4,1)}, u32[]{:S(2)}) copy-start(pred[256]{0:T(512)(128)(4,1)} %get-tuple-element.24) | copy-start | bytes 772
  162.6 3.9 %copy-start.22 = (pred[256]{0:T(512)(128)(4,1)S(1)}, pred[256]{0:T(512)(128)(4,1)}, u32[]{:S(2)}) copy-start(pred[256]{0:T(512)(128)(4,1)} %get-tuple-element.25) | copy-start | bytes 772
  166.3 1.9 copy-start.18
  166.3 1.9 copy-start.19
  168.2 2.5 %copy-start.5 = (bf16[4,256,2048]{2,1,0:T(8,128)(2,1)S(1)}, bf16[4,256,2048]{2,1,0:T(8,128)(2,1)}, u32[]{:S(2)}) copy-start(bf16[4,256,2048]{2,1,0:T(8,128)(2,1)} %param.21) | copy-start | bytes 12582916
  168.2 2.5 %copy-start.16 = (pred[256]{0:T(512)(128)(4,1)S(1)}, pred[256]{0:T(512)(128)(4,1)}, u32[]{:S(2)}) copy-start(pred[256]{0:T(512)(128)(4,1)} %get-tuple-element.20) | copy-start | bytes 772
  168.2 2.5 %copy-start.17 = (pred[256]{0:T(512)(128)(4,1)S(1)}, pred[256]{0:T(512)(128)(4,1)}, u32[]{:S(2)}) copy-start(pred[256]{0:T(512)(128)(4,1)} %get-tuple-element.22) | copy-start | bytes 772
  170.7 0.6 copy-start.23
  170.7 0.7 copy-start.24
  171.3 17.8 %copy-start.1 = (bf16[2,2048,256]{2,1,0:T(8,128)(2,1)S(1)}, bf16[2,2048,256]{2,1,0:T(8,128)(2,1)}, u32[]{:S(2)}) copy-start(bf16[2,2048,256]{2,1,0:T(8,128)(2,1)} %param.20) | copy-start | bytes 6291460
  172.7 8.9 %collective-permute-start.14 = (bf16[64,2048]{1,0:T(8,128)(2,1)}, bf16[64,2048]{1,0:T(8,128)(2,1)}, u32[]{:S(2)}, u32[]{:S(2)}) collective-permute-start(bf16[64,2048]{1,0:T(8,128)(2,1)} %get-tuple-element.42), channel_id=1, source_target_pairs={{0,8},{8,16},{16,24},{24,0},{1,9},{9,17},{17,25},{25,1},{2,10},{10... | collective-permute-start | bytes 786440 | tf_op jit(solution)/shard_map/ppermute | solution.py:102
  172.7 8.9 %collective-permute-start.16 = (bf16[64,2048]{1,0:T(8,128)(2,1)}, bf16[64,2048]{1,0:T(8,128)(2,1)}, u32[]{:S(2)}, u32[]{:S(2)}) collective-permute-start(bf16[64,2048]{1,0:T(8,128)(2,1)} %get-tuple-element.43), channel_id=1, source_target_pairs={{0,24},{8,0},{16,8},{24,16},{1,25},{9,1},{17,9},{25,17},{2,26},{10... | collective-permute-start | bytes 786440 | tf_op jit(solution)/shard_map/ppermute | solution.py:102
  174.4 12.8 %collective-permute-start.15 = (bf16[64,2048]{1,0:T(8,128)(2,1)S(1)}, bf16[64,2048]{1,0:T(8,128)(2,1)}, u32[]{:S(2)}, u32[]{:S(2)}) collective-permute-start(bf16[64,2048]{1,0:T(8,128)(2,1)S(1)} %get-tuple-element.44), channel_id=1, source_target_pairs={{0,16},{8,24},{16,0},{24,8},{1,17},{9,25},{17,1},{25,9},{2,18},{10... | collective-permute-start | bytes 786440 | tf_op jit(solution)/shard_map/ppermute | solution.py:102
Sparse Core Ops, SparseCore 0:
  10.4 19.4 all-gather.1
